TPU v7x, 256 devices: a whole 4x4x8 slice. The times are simulated.
256 devices in a mesh: dp: 32 (over z, y), expert: 8 (over x, core).
Axes of the slice: x: 4, y: 4, z: 8, core: 2. Of those that a mesh axis runs over, the one named last changes fastest.
Arguments:
- residual: bfloat16 [2048, 4096], P(('dp', 'expert')), may hold values from -8.2 to 8.2
- queries: bfloat16 [2048, 4096], P('dp', 'expert'), may hold values from -24 to 24
- new_keys: bfloat16 [2048, 1024], P('dp', 'expert'), may hold values from -6 to 6
- new_values: bfloat16 [2048, 1024], P('dp', 'expert'), may hold values from -6 to 6
- cache_keys: bfloat16 [64, 1024, 1024], P('dp', None, 'expert'), may hold values from -8 to 8
- cache_values: bfloat16 [64, 1024, 1024], P('dp', None, 'expert'), may hold values from -6 to 6
- out_weight: bfloat16 [4096, 4096], P('expert', 'dp'), may hold values from -1 to 1
- ffn_gain: float32 [4096], replicated, may hold values from 0.1 to 1.9
- router: bfloat16 [4096, 8], replicated, may hold values from -0.0234375 to 0.0234375
- routes: int32 [2048, 2], P(('dp', 'expert')), may hold values from 0 to 7, all different within a row; in each aligned block of 64 rows (0 to 63, 64 to 127, ...) at most 24 rows name the same one
- w_gate: bfloat16 [8, 4096, 14336], P('expert', None, 'dp'), may hold values from -0.09375 to 0.09375
- w_up: bfloat16 [8, 4096, 14336], P('expert', None, 'dp'), may hold values from -0.09375 to 0.09375
- w_down: bfloat16 [8, 14336, 4096], P('expert', 'dp'), may hold values from -0.046875 to 0.046875
- summary_gain: float32 [4096], P('expert'), may hold values from 0.1 to 1.9
- reduce_scale: float32 [32], P('expert'), may hold values from 0.1 to 30
- assign: int32 [64], replicated, may hold values from 0 to 3
Outputs:
- summary: bfloat16 [64, 4096], P('dp', 'expert')
- reduced: bfloat16 [64, 4096], P('dp', 'expert')
Inputs may be any that keep to these rules, and one draw needn't show every extreme that they name: `routes`: each token names 2 different experts and every expert is named by some token; among the tokens of one dp index (aligned blocks of 64 rows) no expert is named by more than 24 tokens, and that bound is reached in some block.
All inputs are finite; a program needn't handle non-finite values.
Results may differ from a plain program's by a relative error of at most 0.017.
Values may be sent and summed in bfloat16 or wider, within the bound.
No kernel may reach another device: no remote copies, remote signals or barrier semaphores. Data moves between devices by JAX's collectives and lax.ppermute only.
A program may use at most 128 MiB of HBM per device.

v0:
```python
import math
import jax
import jax.numpy as jnp
from jax import lax
from jax.sharding import PartitionSpec as P

HEADS = 32
KVH = 8
HD = 128
EXPERTS = 8
WIN = 32
GROUP_CAP = 24
EPSILON = 1e-05


def attend(queries, new_keys, new_values, cache_keys, cache_values):
    span_count, cache_len, kv_width = cache_keys.shape
    kv_local = kv_width // HD
    group = HEADS // KVH
    window = queries.shape[0] // span_count
    query_view = queries.reshape(span_count, window, kv_local, group, HD)
    fresh_keys = new_keys.reshape(span_count, window, kv_local, HD)
    fresh_values = new_values.reshape(span_count, window, kv_local, HD)
    stored_keys = cache_keys.reshape(span_count, cache_len, kv_local, HD)
    stored_values = cache_values.reshape(span_count, cache_len, kv_local, HD)
    factor = 1.0 / math.sqrt(HD)
    past_scores = (
        jnp.einsum("ctkgd,cpkd->ckgtp", query_view, stored_keys, preferred_element_type=jnp.float32)
        * factor
    )
    fresh_scores = (
        jnp.einsum("ctkgd,cskd->ckgts", query_view, fresh_keys, preferred_element_type=jnp.float32)
        * factor
    )
    causal = jnp.arange(window)[:, None] >= jnp.arange(window)[None, :]
    fresh_scores = jnp.where(causal, fresh_scores, -jnp.inf)
    highest = jnp.maximum(jnp.max(past_scores, axis=-1), jnp.max(fresh_scores, axis=-1))[..., None]
    past_exp = jnp.exp(past_scores - highest)
    fresh_exp = jnp.exp(fresh_scores - highest)
    totals = jnp.sum(past_exp, axis=-1, keepdims=True) + jnp.sum(fresh_exp, axis=-1, keepdims=True)
    past_weights = (past_exp / totals).astype(jnp.bfloat16)
    fresh_weights = (fresh_exp / totals).astype(jnp.bfloat16)
    context = jnp.einsum(
        "ckgtp,cpkd->ctkgd", past_weights, stored_values, preferred_element_type=jnp.float32
    )
    context = context + jnp.einsum(
        "ckgts,cskd->ctkgd", fresh_weights, fresh_values, preferred_element_type=jnp.float32
    )
    return context.astype(jnp.bfloat16).reshape(span_count * window, kv_local * group * HD)


def shards(
    residual,
    queries,
    new_keys,
    new_values,
    cache_keys,
    cache_values,
    out_weight,
    ffn_gain,
    router,
    routes,
    w_gate,
    w_up,
    w_down,
    summary_gain,
    reduce_scale,
    assign,
):
    expert_count = lax.axis_size("expert")
    dp_index = lax.axis_index("dp")
    column = lax.axis_index("expert")
    span_local = cache_keys.shape[0]
    tok_local = residual.shape[0]
    width = residual.shape[1]
    slice_width = width // expert_count
    highest_precision = lax.Precision.HIGHEST
    attended = attend(queries, new_keys, new_values, cache_keys, cache_values)
    head_terms = jnp.dot(
        attended,
        lax.all_gather(out_weight, "dp", axis=1, tiled=True),
        preferred_element_type=jnp.float32,
    )
    mixed = residual.astype(jnp.float32) + lax.psum_scatter(
        head_terms, "expert", scatter_dimension=0, tiled=True
    )
    normed = (
        mixed * lax.rsqrt(jnp.mean(mixed * mixed, axis=-1, keepdims=True) + EPSILON) * ffn_gain
    ).astype(jnp.bfloat16)
    expert_ids = jnp.arange(EXPERTS, dtype=jnp.int32)
    first = routes[:, 0:1] == expert_ids[None, :]
    second = routes[:, 1:2] == expert_ids[None, :]
    partner = jnp.where(first, routes[:, 1:2], jnp.where(second, routes[:, 0:1], -1))
    outgoing = jnp.where((partner >= 0).T[:, :, None], normed[None, :, :], 0)
    arrived_rows, arrived_partner = (
        lax.all_to_all(outgoing, "expert", split_axis=0, concat_axis=1, tiled=True),
        lax.all_to_all(partner.T, "expert", split_axis=0, concat_axis=1, tiled=True),
    )
    present = (arrived_partner >= 0).astype(jnp.int32)
    position = jnp.cumsum(present, axis=1) - 1
    picker = (present[:, None, :] > 0) & (
        position[:, None, :] == jnp.arange(GROUP_CAP)[None, :, None]
    )
    compact = jnp.einsum(
        "eks,esd->ked",
        picker.astype(jnp.bfloat16),
        arrived_rows,
        preferred_element_type=jnp.float32,
    ).astype(jnp.bfloat16)
    arrived_count = arrived_partner.shape[1]
    pick = picker[0]
    slot_present = jnp.any(pick, axis=1)
    slot_partner = jnp.sum(jnp.where(pick, arrived_partner[0][None, :], 0), axis=1)
    local_span = jnp.arange(arrived_count) // WIN
    slot_span = jnp.sum(jnp.where(pick, local_span[None, :], 0), axis=1)
    slot_logits = jnp.dot(compact[:, 0, :], router, preferred_element_type=jnp.float32)
    own_logit = jnp.sum(jnp.where(expert_ids[None, :] == column, slot_logits, 0.0), axis=-1)
    partner_logit = jnp.sum(
        jnp.where(expert_ids[None, :] == slot_partner[:, None], slot_logits, 0.0), axis=-1
    )
    slot_gate = jnp.where(slot_present, jax.nn.sigmoid(own_logit - partner_logit), 0.0)
    pool_weight = jnp.where(
        slot_span[:, None] == jnp.arange(span_local)[None, :], slot_gate[:, None], 0.0
    )
    gathered = lax.all_gather(compact, "dp", axis=0, tiled=True)
    gathered_weight = lax.all_gather(pool_weight, "dp", axis=0, tiled=True)
    n_dp = gathered.shape[0] // GROUP_CAP
    gate_proj = jnp.einsum("ned,edf->nf", gathered, w_gate, preferred_element_type=jnp.float32)
    up_proj = jnp.einsum("ned,edf->nf", gathered, w_up, preferred_element_type=jnp.float32)
    hidden = (jax.nn.silu(gate_proj) * up_proj).astype(jnp.bfloat16)
    span_hidden = jnp.einsum(
        "iks,ikf->isf",
        gathered_weight.reshape(n_dp, GROUP_CAP, span_local),
        hidden.reshape(n_dp, GROUP_CAP, -1).astype(jnp.float32),
        precision=highest_precision,
    ).reshape(n_dp * span_local, -1)
    pooled_part = jnp.dot(span_hidden, w_down[0].astype(jnp.float32), precision=highest_precision)
    own_span = dp_index * span_local + column * tok_local // WIN
    span_count = n_dp * span_local
    mixed_sum = jnp.sum(mixed, axis=0)
    pooled_part = pooled_part + jnp.where(
        (jnp.arange(span_count) == own_span)[:, None], mixed_sum[None, :], 0.0
    )
    pooled_cols = lax.psum_scatter(pooled_part, "expert", scatter_dimension=1, tiled=True)
    pooled_cols = lax.psum(pooled_cols, "dp")
    squares = lax.psum(jnp.sum(pooled_cols * pooled_cols, axis=-1), "expert")
    everyone = (pooled_cols * lax.rsqrt(squares / width + EPSILON)[:, None] * summary_gain).astype(
        jnp.bfloat16
    )
    summary = lax.dynamic_slice_in_dim(everyone, dp_index * span_local, span_local)
    heads_local = slice_width // HD
    mine = summary.reshape(span_local, heads_local, HD)
    others = everyone.reshape(everyone.shape[0], heads_local, HD)
    factor = reduce_scale / math.sqrt(HD)
    scores = (
        jnp.einsum("chd,khd->hck", mine, others, preferred_element_type=jnp.float32)
        * factor[:, None, None]
    )
    own_assign = lax.dynamic_slice_in_dim(assign, dp_index * span_local, span_local)
    same = own_assign[:, None] == assign[None, :]
    scores = jnp.where(same[None], scores, -jnp.inf)
    highest = jnp.max(scores, axis=-1, keepdims=True)
    expo = jnp.exp(scores - highest)
    weights = (expo / jnp.sum(expo, axis=-1, keepdims=True)).astype(jnp.bfloat16)
    reduced = jnp.einsum("hck,khd->chd", weights, others, preferred_element_type=jnp.float32)
    reduced = reduced.reshape(span_local, slice_width).astype(jnp.bfloat16)
    return (summary, reduced)


def solution(mesh):
    return jax.shard_map(
        shards,
        mesh=mesh,
        in_specs=(
            P(("dp", "expert"), None),
            P("dp", "expert"),
            P("dp", "expert"),
            P("dp", "expert"),
            P("dp", None, "expert"),
            P("dp", None, "expert"),
            P("expert", "dp"),
            P(),
            P(),
            P(("dp", "expert"), None),
            P("expert", None, "dp"),
            P("expert", None, "dp"),
            P("expert", "dp", None),
            P("expert"),
            P("expert"),
            P(),
        ),
        out_specs=(P("dp", "expert"), P("dp", "expert")),
        check_vma=False,
    )
```

profile of v0, /device:TPU:1, one launch (start us, length us, event | category | flops | bytes accessed | tf_op | source)
XLA Modules:
  0.0 459.1 jit_solution(10144320645197838944)
XLA Ops:
  7.2 0.7 all-gather.4.cloned.1.call-update
  8.0 0.9 reshape.501
  9.2 1.0 fusion.60
  10.6 0.9 fusion.40
  11.5 0.4 fusion.22
  12.0 82.2 %all-gather.4.cloned.1.call-done = bf16[512,4096]{1,0:T(8,128)(2,1)} async-done(((bf16[512,128]{1,0:T(8,128)(2,1)}), bf16[512,4096]{1,0:T(8,128)(2,1)}) %all-gather.4.cloned.1.call-update) | async-done | bytes 4194320 | tf_op jit(solution)/shard_map/all_gather | solution.py:81
  94.2 4.0 fusion.35
  98.3 0.6 compare_select_fusion.1
  98.9 7.7 %all-to-all-start = ((s32[8,1,8]{2,1,0:T(1,128)}), s32[8,1,8]{2,1,0:T(1,128)S(1)}, u32[]{:S(2)}, u32[]{:S(2)}) async-start(s32[8,1,8]{2,1,0:T(1,128)} %compare_select_fusion.1), calls=%async_computation | async-start | bytes 8192 | tf_op jit(solution)/shard_map/all_to_all | solution.py:97
  106.6 27.6 %reduce-scatter.3.cloned.1.call-done = f32[8,4096]{1,0:T(8,128)} async-done(((f32[64,4096]{1,0:T(8,128)}), f32[8,4096]{1,0:T(8,128)}) %reduce-scatter.3.cloned.1.call-update) | async-done | bytes 131088 | tf_op jit(solution)/shard_map/reduce_scatter | solution.py:84
  134.2 1.1 fusion.47
  135.3 1.0 multiply_convert_fusion.1
  136.3 0.9 broadcast_select_fusion
  137.2 6.3 %all-to-all-start.1 = ((bf16[8,8,4096]{2,1,0:T(8,128)(2,1)}), bf16[8,8,4096]{2,1,0:T(8,128)(2,1)S(1)}, u32[]{:S(2)}, u32[]{:S(2)}) async-start(bf16[8,8,4096]{2,1,0:T(8,128)(2,1)} %broadcast_select_fusion), calls=%async_computation.2 | async-start | bytes 1048576 | tf_op jit(solution)/shard_map/all_to_all | solution.py:96
  143.5 0.5 broadcast.319
  144.0 0.7 fusion.58
  145.1 7.8 %all-to-all-done.1 = bf16[8,8,4096]{2,1,0:T(8,128)(2,1)S(1)} async-done(((bf16[8,8,4096]{2,1,0:T(8,128)(2,1)}), bf16[8,8,4096]{2,1,0:T(8,128)(2,1)S(1)}, u32[]{:S(2)}, u32[]{:S(2)}) %all-to-all-start.1) | async-done | bytes 524320 | tf_op jit(solution)/shard_map/all_to_all | solution.py:96
  152.9 0.9 convolution_convert_fusion
  154.2 1.1 select_reduce_fusion.2
  155.3 36.3 %all-gather = f32[32,24,2]{1,2,0:T(2,128)S(1)} all-gather(f32[1,24,2]{1,2,0:T(2,128)S(1)} %fusion.56), channel_id=1, replica_groups=mesh['dp'=32,'expert'=8] {'dp'}, dimensions={0}, use_global_device_ids=true | all-gather | bytes 6336 | tf_op jit(solution)/shard_map/all_gather | solution.py:126
  191.6 49.7 %all-gather.6.cloned.1.call-done = bf16[768,1,4096]{2,0,1:T(8,128)(2,1)} async-done(((bf16[24,1,4096]{2,0,1:T(8,128)(2,1)}), bf16[768,1,4096]{2,0,1:T(8,128)(2,1)}) %all-gather.6.cloned.1.call-update) | async-done | bytes 6291472 | tf_op jit(solution)/shard_map/all_gather | solution.py:125
  241.3 7.0 %fusion.3 = f32[768,448]{0,1:T(8,128)S(1)} fusion(bf16[768,1,4096]{2,0,1:T(8,128)(2,1)} %all-gather.6.cloned.1.call-done, bf16[1,4096,448]{1,2,0:T(8,128)(2,1)} %param.26), kind=kOutput, calls=%fused_computation.3 | convolution fusion | flops 2818572288 | bytes 11337728 | tf_op jit(solution)/shard_map/ned,edf->nf/dot_general | solution.py:128
  248.4 3.1 fusion.14
  251.8 0.5 fusion.66
  252.4 5.1 %convolution_add_fusion = f32[64,4096]{1,0:T(8,128)} fusion(f32[64,448]{1,0:T(8,128)S(1)} %reshape.513, bf16[1,448,4096]{2,1,0:T(8,128)(2,1)} %param.28, f32[4096]{0:T(1024)S(1)} %get-tuple-element.2, pred[64]{0:T(512)(128)(4,1)S(1)} %iota_compare_fusion.5), kind=kOutput, calls=%fused_computation.5 | convolution fusion | flops 1409810432 | bytes 4849728 | tf_op jit(solution)/shard_map/dot_general | solution.py:137
  257.8 30.3 %reduce-scatter.5.cloned.1.call-done = f32[64,512]{1,0:T(8,128)} async-done(((f32[64,4096]{1,0:T(8,128)}), f32[64,512]{1,0:T(8,128)}) %reduce-scatter.5.cloned.1.call-update) | async-done | bytes 131088 | tf_op jit(solution)/shard_map/reduce_scatter | solution.py:144
  288.1 142.7 %all-reduce.2.cloned.1.call-done = f32[64,512]{1,0:T(8,128)} async-done(((f32[64,512]{1,0:T(8,128)}), f32[64,512]{1,0:T(8,128)}) %all-reduce.2.cloned.1.call-update) | async-done | bytes 131088 | tf_op jit(solution)/shard_map/psum | solution.py:145
  430.8 1.0 multiply_reduce_fusion
  431.8 16.7 %psum.15 = f32[64]{0:T(128)S(1)} all-reduce(f32[64]{0:T(128)S(1)} %multiply_reduce_fusion), channel_id=1, replica_groups=mesh['dp'=32,'expert'=8] {'expert'}, use_global_device_ids=true, to_apply=%region_16.17 | all-reduce | flops 64 | bytes 512 | tf_op jit(solution)/shard_map/psum | solution.py:146
  448.6 1.0 multiply_convert_fusion
  449.6 1.3 fusion.61
  450.9 1.7 fusion.26
  (63 shorter events, 2.3 us)
Async XLA Ops:
  7.2 1.7 copy-start
  7.2 4.3 copy-start.8
  7.2 87.0 %all-gather.4.cloned.1.call-start = ((), (), s32[]{:S(2)}) async-start(), calls=%async_computation.4 | async-start | bytes 4325376 | tf_op jit(solution)/shard_map/all_gather | solution.py:81
  7.9 126.3 %reduce-scatter.3.cloned.1.call-start = ((), (), s32[]{:S(2)}) async-start(), calls=%async_computation.5 | async-start | bytes 1179648 | tf_op jit(solution)/shard_map/reduce_scatter | solution.py:84
  11.9 86.4 %copy-start.5 = (s32[8,2]{0,1:T(2,128)S(1)}, s32[8,2]{0,1:T(2,128)}, u32[]{:S(2)}) copy-start(s32[8,2]{0,1:T(2,128)} %param.25) | copy-start | bytes 196
  11.9 122.3 %copy-start.1 = (bf16[8,4096]{1,0:T(8,128)(2,1)S(1)}, bf16[8,4096]{1,0:T(8,128)(2,1)}, u32[]{:S(2)}) copy-start(bf16[8,4096]{1,0:T(8,128)(2,1)} %param.16) | copy-start | bytes 196612
  11.9 123.4 %copy-start.2 = (f32[4096]{0:T(1024)S(1)}, f32[4096]{0:T(1024)}, u32[]{:S(2)}) copy-start(f32[4096]{0:T(1024)} %param.23) | copy-start | bytes 49156
  94.2 59.9 %copy-start.9 = (bf16[4096,8]{0,1:T(8,128)(2,1)S(1)}, bf16[4096,8]{0,1:T(8,128)(2,1)}, u32[]{:S(2)}) copy-start(bf16[4096,8]{0,1:T(8,128)(2,1)} %param.24) | copy-start | bytes 196612
  98.9 38.3 %all-to-all-start = ((s32[8,1,8]{2,1,0:T(1,128)}), s32[8,1,8]{2,1,0:T(1,128)S(1)}, u32[]{:S(2)}, u32[]{:S(2)}) async-start(s32[8,1,8]{2,1,0:T(1,128)} %compare_select_fusion.1), calls=%async_computation | async-start | bytes 8192 | tf_op jit(solution)/shard_map/all_to_all | solution.py:97
  137.2 15.7 %all-to-all-start.1 = ((bf16[8,8,4096]{2,1,0:T(8,128)(2,1)}), bf16[8,8,4096]{2,1,0:T(8,128)(2,1)S(1)}, u32[]{:S(2)}, u32[]{:S(2)}) async-start(bf16[8,8,4096]{2,1,0:T(8,128)(2,1)} %broadcast_select_fusion), calls=%async_computation.2 | async-start | bytes 1048576 | tf_op jit(solution)/shard_map/all_to_all | solution.py:96
  143.5 97.8 %all-gather.6.cloned.1.call-start = ((), (), s32[]{:S(2)}) async-start(), calls=%async_computation.6 | async-start | bytes 6488064 | tf_op jit(solution)/shard_map/all_gather | solution.py:125
  153.8 134.2 %reduce-scatter.5.cloned.1.call-start = ((), (), s32[]{:S(2)}) async-start(), calls=%async_computation.7 | async-start | bytes 1179648 | tf_op jit(solution)/shard_map/reduce_scatter | solution.py:144
  241.3 7.1 %copy-start.6 = (bf16[768,1,4096]{2,0,1:T(8,128)(2,1)S(1)}, bf16[768,1,4096]{2,0,1:T(8,128)(2,1)}, u32[]{:S(2)}) copy-start(bf16[768,1,4096]{2,0,1:T(8,128)(2,1)} %all-gather.6.cloned.1.call-done) | copy-start | bytes 18874372
  241.3 7.1 %copy-start.7 = (bf16[1,4096,448]{1,2,0:T(8,128)(2,1)S(1)}, bf16[1,4096,448]{1,2,0:T(8,128)(2,1)}, u32[]{:S(2)}) copy-start(bf16[1,4096,448]{1,2,0:T(8,128)(2,1)} %param.27) | copy-start | bytes 11010052
  251.8 5.8 %copy-start.10 = (s32[64]{0:T(128)S(1)}, s32[64]{0:T(128)}, u32[]{:S(2)}) copy-start(s32[64]{0:T(128)} %param.31) | copy-start | bytes 772
  251.8 36.3 %copy-start.11 = (f32[4]{0:T(128)S(1)}, f32[4]{0:T(128)}, u32[]{:S(2)}) copy-start(f32[4]{0:T(128)} %param.30) | copy-start | bytes 52
  251.8 196.8 %copy-start.3 = (f32[512]{0:T(512)S(1)}, f32[512]{0:T(512)}, u32[]{:S(2)}) copy-start(f32[512]{0:T(512)} %param.29) | copy-start | bytes 6148
  257.5 173.3 %all-reduce.2.cloned.1.call-start = ((), (), s32[]{:S(2)}) async-start(), calls=%async_computation.8 | async-start | bytes 262144 | tf_op jit(solution)/shard_map/psum | solution.py:145
  449.6 3.0 copy-start.4
Sparse Core Ops, SparseCore 0:
  10.5 83.7 all-gather.3
  98.4 35.7 reduce-scatter.2
  153.9 87.3 all-gather.5
  257.7 30.3 reduce-scatter.4
  291.3 139.4 all-reduce.1
where the time goes:
time: 460 us; the launch traced here: 459 us
  waiting for transfers between devices  341 us (74%)
  blocking collectives  53 us (12%)
  matrix products  27.4 us (6%)
  starting transfers between devices  14.2 us (3%)
  between operations  14.1 us (3%)
  other arithmetic  7.17 us (2%)
    psum x1, waiting for transfers between devices, shards(): pooled_cols = lax.psum(pooled_cols, 'dp')  143 us
    all_gather x1, waiting for transfers between devices, shards(): lax.all_gather(out_weight, 'dp', axis=1, tiled=True)  82.2 us
    all_gather x1, waiting for transfers between devices, shards(): gathered = lax.all_gather(compact, 'dp', axis=0, tiled=True)  49.7 us
    all_gather x1, blocking collectives, shards(): gathered_weight = lax.all_gather(pool_weight, 'dp', axis=0, tiled=True)  36.3 us
    reduce_scatter x1, waiting for transfers between devices, shards(): lax.psum_scatter(pooled_part, 'expert', scatter_dimension=1, tiled=True)  30.3 us
    reduce_scatter x1, waiting for transfers between devices, shards(): lax.psum_scatter(head_terms, 'expert', scatter_dimension=0, tiled=True)  27.6 us
    psum x1, blocking collectives, shards(): squares = lax.psum(jnp.sum(pooled_cols * pooled_cols, axis=-1), 'expert')  16.7 us
  transfers between devices with their start and end apart: 7, of which 6 were waited for; matrix products, arithmetic and copies ran while one was open for 2% of the time, Pallas kernels for 0%

commit v1 on v0

--- a/solution.py
+++ b/solution.py
@@ -3,6 +3,7 @@
 import jax.numpy as jnp
 from jax import lax
 from jax.sharding import PartitionSpec as P
+from jax.lax import ppermute, psum
 
 HEADS = 32
 KVH = 8
@@ -142,7 +143,19 @@
         (jnp.arange(span_count) == own_span)[:, None], mixed_sum[None, :], 0.0
     )
     pooled_cols = lax.psum_scatter(pooled_part, "expert", scatter_dimension=1, tiled=True)
-    pooled_cols = lax.psum(pooled_cols, "dp")
+
+    def screen_find(mine_x, a_name):
+        num_devices = psum(1, a_name)
+        base_arr = mine_x
+        for k in [
+            [(num, num ^ p) for num in range(num_devices)]
+            for p in (1, 2, 4, 8, 16)
+            if p < num_devices
+        ]:
+            base_arr = base_arr + ppermute(base_arr, a_name, perm=k)
+        return base_arr
+
+    pooled_cols = screen_find(pooled_cols, "dp")
     squares = lax.psum(jnp.sum(pooled_cols * pooled_cols, axis=-1), "expert")
     everyone = (pooled_cols * lax.rsqrt(squares / width + EPSILON)[:, None] * summary_gain).astype(
         jnp.bfloat16

time: 460 us -> 350 us (0.76)
  waiting for transfers between devices: 341 us -> 214 us
  starting transfers between devices: 14.2 us -> 26.7 us
  blocking collectives: 53 us -> 59.9 us
    psum x1 -> x0, waiting for transfers between devices: 143 us -> none  [shards(): pooled_cols = lax.psum(pooled_cols, 'dp')]
    ppermute x0 -> x5, waiting for transfers between devices: none -> 15.7 us  [screen_find(): base_arr = base_arr + ppermute(base_arr, a_name, perm=k)]
    ppermute x0 -> x5, starting transfers between devices: none -> 12.6 us  [screen_find(): base_arr = base_arr + ppermute(base_arr, a_name, perm=k)]
    psum x1, blocking collectives: 16.7 us -> 23.6 us  [shards(): squares = lax.psum(jnp.sum(pooled_cols * pooled_cols, axis=-1), 'expert')]
  transfers between devices with their start and end apart: 7 -> 11, of which waited for: 6 -> 10; matrix products, arithmetic and copies ran while one was open for 2% -> 3% of each run, Pallas kernels for 0% -> 0%
where the time goes in v1:
time: 350 us; the launch traced here: 349 us
  waiting for transfers between devices  214 us (61%)
  blocking collectives  59.9 us (17%)
  starting transfers between devices  26.7 us (8%)
  matrix products  25.6 us (7%)
  between operations  14.1 us (4%)
  other arithmetic  6.35 us (2%)
    all_gather x1, waiting for transfers between devices, shards(): lax.all_gather(out_weight, 'dp', axis=1, tiled=True)  82.2 us
    all_gather x1, waiting for transfers between devices, shards(): gathered = lax.all_gather(compact, 'dp', axis=0, tiled=True)  49.7 us
    all_gather x1, blocking collectives, shards(): gathered_weight = lax.all_gather(pool_weight, 'dp', axis=0, tiled=True)  36.3 us
    reduce_scatter x1, waiting for transfers between devices, shards(): lax.psum_scatter(pooled_part, 'expert', scatter_dimension=1, tiled=True)  30.5 us
    reduce_scatter x1, waiting for transfers between devices, shards(): lax.psum_scatter(head_terms, 'expert', scatter_dimension=0, tiled=True)  27.6 us
    psum x1, blocking collectives, shards(): squares = lax.psum(jnp.sum(pooled_cols * pooled_cols, axis=-1), 'expert')  23.6 us
    ppermute x5, waiting for transfers between devices, screen_find(): base_arr = base_arr + ppermute(base_arr, a_name, perm=k)  15.7 us
    ppermute x5, starting transfers between devices, screen_find(): base_arr = base_arr + ppermute(base_arr, a_name, perm=k)  12.6 us
  transfers between devices with their start and end apart: 11, of which 10 were waited for; matrix products, arithmetic and copies ran while one was open for 3% of the time, Pallas kernels for 0%

profile of v1, /device:TPU:1, one launch (start us, length us, event | category | flops | bytes accessed | tf_op | source)
XLA Modules:
  0.0 349.0 jit_solution(8707688940483696549)
XLA Ops:
  8.0 0.9 reshape.501
  9.2 1.0 fusion.60
  10.6 0.9 fusion.40
  12.0 82.2 %all-gather.4.cloned.1.call-done = bf16[512,4096]{1,0:T(8,128)(2,1)} async-done(((bf16[512,128]{1,0:T(8,128)(2,1)}), bf16[512,4096]{1,0:T(8,128)(2,1)}) %all-gather.4.cloned.1.call-update) | async-done | bytes 4194320 | tf_op jit(solution)/shard_map/all_gather | solution.py:82
  94.2 4.0 %fusion.35 = f32[64,4096]{1,0:T(8,128)} fusion(bf16[512,4096]{1,0:T(8,128)(2,1)} %all-gather.4.cloned.1.call-done, bf16[8,8,4,128]{3,2,1,0:T(4,128)(2,1)S(1)} %bitcast.123), kind=kOutput, calls=%fused_computation.44 | convolution fusion | flops 268435456 | bytes 5308416 | tf_op jit(solution)/shard_map/dot_general | solution.py:80
  98.9 7.7 %all-to-all-start = ((s32[8,1,8]{2,1,0:T(1,128)}), s32[8,1,8]{2,1,0:T(1,128)S(1)}, u32[]{:S(2)}, u32[]{:S(2)}) async-start(s32[8,1,8]{2,1,0:T(1,128)} %compare_select_fusion.1), calls=%async_computation | async-start | bytes 8192 | tf_op jit(solution)/shard_map/all_to_all | solution.py:98
  106.6 27.6 %reduce-scatter.3.cloned.1.call-done = f32[8,4096]{1,0:T(8,128)} async-done(((f32[64,4096]{1,0:T(8,128)}), f32[8,4096]{1,0:T(8,128)}) %reduce-scatter.3.cloned.1.call-update) | async-done | bytes 131088 | tf_op jit(solution)/shard_map/reduce_scatter | solution.py:85
  134.2 1.1 fusion.47
  135.3 1.0 multiply_convert_fusion.1
  136.3 0.9 broadcast_select_fusion
  137.2 6.3 %all-to-all-start.1 = ((bf16[8,8,4096]{2,1,0:T(8,128)(2,1)}), bf16[8,8,4096]{2,1,0:T(8,128)(2,1)S(1)}, u32[]{:S(2)}, u32[]{:S(2)}) async-start(bf16[8,8,4096]{2,1,0:T(8,128)(2,1)} %broadcast_select_fusion), calls=%async_computation.2 | async-start | bytes 1048576 | tf_op jit(solution)/shard_map/all_to_all | solution.py:97
  145.1 7.8 %all-to-all-done.1 = bf16[8,8,4096]{2,1,0:T(8,128)(2,1)S(1)} async-done(((bf16[8,8,4096]{2,1,0:T(8,128)(2,1)}), bf16[8,8,4096]{2,1,0:T(8,128)(2,1)S(1)}, u32[]{:S(2)}, u32[]{:S(2)}) %all-to-all-start.1) | async-done | bytes 524320 | tf_op jit(solution)/shard_map/all_to_all | solution.py:97
  152.9 0.9 convolution_convert_fusion
  154.2 1.1 select_reduce_fusion.2
  155.3 36.3 %all-gather = f32[32,24,2]{1,2,0:T(2,128)S(1)} all-gather(f32[1,24,2]{1,2,0:T(2,128)S(1)} %fusion.56), channel_id=1, replica_groups=mesh['dp'=32,'expert'=8] {'dp'}, dimensions={0}, use_global_device_ids=true | all-gather | bytes 6336 | tf_op jit(solution)/shard_map/all_gather | solution.py:127
  191.6 49.7 %all-gather.6.cloned.1.call-done = bf16[768,1,4096]{2,0,1:T(8,128)(2,1)} async-done(((bf16[24,1,4096]{2,0,1:T(8,128)(2,1)}), bf16[768,1,4096]{2,0,1:T(8,128)(2,1)}) %all-gather.6.cloned.1.call-update) | async-done | bytes 6291472 | tf_op jit(solution)/shard_map/all_gather | solution.py:126
  241.3 7.0 %fusion.3 = f32[768,448]{0,1:T(8,128)S(1)} fusion(bf16[768,1,4096]{2,0,1:T(8,128)(2,1)} %all-gather.6.cloned.1.call-done, bf16[1,4096,448]{1,2,0:T(8,128)(2,1)} %param.26), kind=kOutput, calls=%fused_computation.3 | convolution fusion | flops 2818572288 | bytes 11337728 | tf_op jit(solution)/shard_map/ned,edf->nf/dot_general | solution.py:129
  248.4 3.1 fusion.14
  252.4 5.1 %convolution_add_fusion = f32[64,4096]{1,0:T(8,128)} fusion(f32[64,448]{1,0:T(8,128)S(1)} %reshape.513, bf16[1,448,4096]{2,1,0:T(8,128)(2,1)} %param.28, f32[4096]{0:T(1024)S(1)} %get-tuple-element.2, pred[64]{0:T(512)(128)(4,1)S(1)} %iota_compare_fusion.5), kind=kOutput, calls=%fused_computation.5 | convolution fusion | flops 1409810432 | bytes 4849728 | tf_op jit(solution)/shard_map/dot_general | solution.py:138
  257.5 30.5 %reduce-scatter.5.cloned.1.call-done = f32[64,512]{1,0:T(8,128)} async-done(((f32[64,4096]{1,0:T(8,128)}), f32[64,512]{1,0:T(8,128)}) %reduce-scatter.5.cloned.1.call-update) | async-done | bytes 131088 | tf_op jit(solution)/shard_map/reduce_scatter | solution.py:145
  288.0 0.9 collective-permute-start
  288.9 3.2 collective-permute-done
  292.1 0.9 add.95
  293.0 2.5 collective-permute-start.1
  295.5 3.5 collective-permute-done.1
  299.0 1.4 collective-permute-start.2
  300.4 2.8 collective-permute-done.2
  303.2 2.3 collective-permute-start.3
  305.6 3.8 %collective-permute-done.3 = f32[64,512]{1,0:T(8,128)S(1)} collective-permute-done((f32[64,512]{1,0:T(8,128)S(1)}, f32[64,512]{1,0:T(8,128)S(1)}, u32[]{:S(2)}, u32[]{:S(2)}) %collective-permute-start.3) | collective-permute-done | bytes 131104 | tf_op jit(solution)/shard_map/ppermute | solution.py:155
  309.4 5.5 %collective-permute-start.4 = (f32[64,512]{1,0:T(8,128)S(1)}, f32[64,512]{1,0:T(8,128)S(1)}, u32[]{:S(2)}, u32[]{:S(2)}) collective-permute-start(f32[64,512]{1,0:T(8,128)S(1)} %add.98), channel_id=1, source_target_pairs={{0,128},{8,136},{16,144},{24,152},{32,160},{40,168},{48,176},{56,1... | collective-permute-start | bytes 393224 | tf_op jit(solution)/shard_map/ppermute | solution.py:155
  315.0 2.5 collective-permute-done.4
  317.6 23.6 %psum.7 = f32[64]{0:T(128)S(1)} all-reduce(f32[64]{0:T(128)S(1)} %get-tuple-element.10), channel_id=1, replica_groups=mesh['dp'=32,'expert'=8] {'expert'}, use_global_device_ids=true, to_apply=%region_15.16 | all-reduce | flops 64 | bytes 512 | tf_op jit(solution)/shard_map/psum | solution.py:159
  (74 shorter events, 7.0 us)
Async XLA Ops:
  7.2 1.7 copy-start
  7.2 4.3 %copy-start.8 = (bf16[2,1024,128]{2,1,0:T(8,128)(2,1)S(1)}, bf16[2,1024,128]{2,1,0:T(8,128)(2,1)}, u32[]{:S(2)}) copy-start(bf16[2,1024,128]{2,1,0:T(8,128)(2,1)} %param.21) | copy-start | bytes 1572868
  7.2 87.0 %all-gather.4.cloned.1.call-start = ((), (), s32[]{:S(2)}) async-start(), calls=%async_computation.4 | async-start | bytes 4325376 | tf_op jit(solution)/shard_map/all_gather | solution.py:82
  7.9 126.3 %reduce-scatter.3.cloned.1.call-start = ((), (), s32[]{:S(2)}) async-start(), calls=%async_computation.5 | async-start | bytes 1179648 | tf_op jit(solution)/shard_map/reduce_scatter | solution.py:85
  11.9 86.4 %copy-start.5 = (s32[8,2]{0,1:T(2,128)S(1)}, s32[8,2]{0,1:T(2,128)}, u32[]{:S(2)}) copy-start(s32[8,2]{0,1:T(2,128)} %param.25) | copy-start | bytes 196
  11.9 122.3 %copy-start.1 = (bf16[8,4096]{1,0:T(8,128)(2,1)S(1)}, bf16[8,4096]{1,0:T(8,128)(2,1)}, u32[]{:S(2)}) copy-start(bf16[8,4096]{1,0:T(8,128)(2,1)} %param.16) | copy-start | bytes 196612
  11.9 123.4 %copy-start.2 = (f32[4096]{0:T(1024)S(1)}, f32[4096]{0:T(1024)}, u32[]{:S(2)}) copy-start(f32[4096]{0:T(1024)} %param.23) | copy-start | bytes 49156
  94.2 59.9 %copy-start.9 = (bf16[4096,8]{0,1:T(8,128)(2,1)S(1)}, bf16[4096,8]{0,1:T(8,128)(2,1)}, u32[]{:S(2)}) copy-start(bf16[4096,8]{0,1:T(8,128)(2,1)} %param.24) | copy-start | bytes 196612
  98.9 38.3 %all-to-all-start = ((s32[8,1,8]{2,1,0:T(1,128)}), s32[8,1,8]{2,1,0:T(1,128)S(1)}, u32[]{:S(2)}, u32[]{:S(2)}) async-start(s32[8,1,8]{2,1,0:T(1,128)} %compare_select_fusion.1), calls=%async_computation | async-start | bytes 8192 | tf_op jit(solution)/shard_map/all_to_all | solution.py:98
  137.2 15.7 %all-to-all-start.1 = ((bf16[8,8,4096]{2,1,0:T(8,128)(2,1)}), bf16[8,8,4096]{2,1,0:T(8,128)(2,1)S(1)}, u32[]{:S(2)}, u32[]{:S(2)}) async-start(bf16[8,8,4096]{2,1,0:T(8,128)(2,1)} %broadcast_select_fusion), calls=%async_computation.2 | async-start | bytes 1048576 | tf_op jit(solution)/shard_map/all_to_all | solution.py:97
  143.5 97.8 %all-gather.6.cloned.1.call-start = ((), (), s32[]{:S(2)}) async-start(), calls=%async_computation.6 | async-start | bytes 6488064 | tf_op jit(solution)/shard_map/all_gather | solution.py:126
  153.8 134.2 %reduce-scatter.5.cloned.1.call-start = ((), (), s32[]{:S(2)}) async-start(), calls=%async_computation.7 | async-start | bytes 1179648 | tf_op jit(solution)/shard_map/reduce_scatter | solution.py:145
  241.3 7.1 %copy-start.6 = (bf16[768,1,4096]{2,0,1:T(8,128)(2,1)S(1)}, bf16[768,1,4096]{2,0,1:T(8,128)(2,1)}, u32[]{:S(2)}) copy-start(bf16[768,1,4096]{2,0,1:T(8,128)(2,1)} %all-gather.6.cloned.1.call-done) | copy-start | bytes 18874372
  241.3 7.1 %copy-start.7 = (bf16[1,4096,448]{1,2,0:T(8,128)(2,1)S(1)}, bf16[1,4096,448]{1,2,0:T(8,128)(2,1)}, u32[]{:S(2)}) copy-start(bf16[1,4096,448]{1,2,0:T(8,128)(2,1)} %param.27) | copy-start | bytes 11010052
  252.3 48.0 %copy-start.10 = (s32[64]{0:T(128)S(1)}, s32[64]{0:T(128)}, u32[]{:S(2)}) copy-start(s32[64]{0:T(128)} %param.31) | copy-start | bytes 772
  252.4 62.5 %copy-start.11 = (f32[4]{0:T(128)S(1)}, f32[4]{0:T(128)}, u32[]{:S(2)}) copy-start(f32[4]{0:T(128)} %param.30) | copy-start | bytes 52
  252.4 88.8 %copy-start.3 = (f32[512]{0:T(512)S(1)}, f32[512]{0:T(512)}, u32[]{:S(2)}) copy-start(f32[512]{0:T(512)} %param.29) | copy-start | bytes 6148
  288.0 4.0 %collective-permute-start = (f32[64,512]{1,0:T(8,128)}, f32[64,512]{1,0:T(8,128)S(1)}, u32[]{:S(2)}, u32[]{:S(2)}) collective-permute-start(f32[64,512]{1,0:T(8,128)} %reduce-scatter.5.cloned.1.call-done), channel_id=1, source_target_pairs={{0,8},{8,0},{16,24},{24,16},{32,40},{40,32},{48,56},{56,48},{64,72... | collective-permute-start | bytes 393224 | tf_op jit(solution)/shard_map/ppermute | solution.py:155
  293.0 6.0 %collective-permute-start.1 = (f32[64,512]{1,0:T(8,128)S(1)}, f32[64,512]{1,0:T(8,128)S(1)}, u32[]{:S(2)}, u32[]{:S(2)}) collective-permute-start(f32[64,512]{1,0:T(8,128)S(1)} %add.95), channel_id=1, source_target_pairs={{0,16},{8,24},{16,0},{24,8},{32,48},{40,56},{48,32},{56,40},{64,80... | collective-permute-start | bytes 393224 | tf_op jit(solution)/shard_map/ppermute | solution.py:155
  299.0 4.2 %collective-permute-start.2 = (f32[64,512]{1,0:T(8,128)S(1)}, f32[64,512]{1,0:T(8,128)S(1)}, u32[]{:S(2)}, u32[]{:S(2)}) collective-permute-start(f32[64,512]{1,0:T(8,128)S(1)} %add.96), channel_id=1, source_target_pairs={{0,32},{8,40},{16,48},{24,56},{32,0},{40,8},{48,16},{56,24},{64,96... | collective-permute-start | bytes 393224 | tf_op jit(solution)/shard_map/ppermute | solution.py:155
  303.2 6.2 %collective-permute-start.3 = (f32[64,512]{1,0:T(8,128)S(1)}, f32[64,512]{1,0:T(8,128)S(1)}, u32[]{:S(2)}, u32[]{:S(2)}) collective-permute-start(f32[64,512]{1,0:T(8,128)S(1)} %add.97), channel_id=1, source_target_pairs={{0,64},{8,72},{16,80},{24,88},{32,96},{40,104},{48,112},{56,120},{... | collective-permute-start | bytes 393224 | tf_op jit(solution)/shard_map/ppermute | solution.py:155
  309.4 8.1 %collective-permute-start.4 = (f32[64,512]{1,0:T(8,128)S(1)}, f32[64,512]{1,0:T(8,128)S(1)}, u32[]{:S(2)}, u32[]{:S(2)}) collective-permute-start(f32[64,512]{1,0:T(8,128)S(1)} %add.98), channel_id=1, source_target_pairs={{0,128},{8,136},{16,144},{24,152},{32,160},{40,168},{48,176},{56,1... | collective-permute-start | bytes 393224 | tf_op jit(solution)/shard_map/ppermute | solution.py:155
  341.3 1.2 copy-start.4
Sparse Core Ops, SparseCore 0:
  10.5 83.7 all-gather.3
  98.4 35.7 reduce-scatter.2
  153.9 87.3 all-gather.5
  257.7 30.3 reduce-scatter.4
